TPU v7x, 256 devices: a whole 4x4x8 slice. The times are simulated.
256 devices in a mesh: fsdp: 16 (over z_hi, x), tensor: 16 (over z_lo, y, core).
Axes of the slice: x: 4, y: 4, z: 8 (z_hi: 4, z_lo: 2; z = z_hi * 2 + z_lo), core: 2. Of those that a mesh axis runs over, the one named last changes fastest.
Arguments:
- tokens: bfloat16 [8192, 3072], P('fsdp'), may hold values from -6 to 6
- weights: bfloat16 [3072, 4, 4096], P('fsdp', None, 'tensor'), may hold values from -0.109375 to 0.109375
- direction: bfloat16 [3072, 4, 4096], P('fsdp', None, 'tensor'), may hold values from -0.109375 to 0.109375
- precision: float32 [3072], replicated, may hold values from 0.25 to 4
Outputs:
- ggn: float32 [3072, 4, 4096], P('fsdp', None, 'tensor')
All inputs are finite; a program needn't handle non-finite values.
Results may differ from a plain program's by a relative error of at most 0.015.
Values may be sent and summed in bfloat16 or wider, within the bound.
No kernel may reach another device: no remote copies, remote signals or barrier semaphores. Data moves between devices by JAX's collectives and lax.ppermute only.
A program may use at most 128 MiB of HBM per device.

v0:
```python
import jax
import jax.numpy as jnp
from jax import lax
from jax.sharding import Mesh, PartitionSpec as P

FSDP = ("z_hi", "x")
TENSOR = ("z_lo", "y", "core")
HEAD = 128
PATCHES = 256


def layer_norm(rows):
    mean_row = jnp.mean(rows, -1, keepdims=True)
    centred = rows - mean_row
    spread = jnp.mean(centred * centred, -1, keepdims=True)
    return centred * lax.rsqrt(spread + 1e-06)


def attend(queries, key_rows, value_rows):
    query_norm = layer_norm(queries)
    key_norm = layer_norm(key_rows)
    score_scale = queries.shape[-1] ** (-0.5)
    scores = (
        jnp.einsum("bqhe,bkhe->bhqk", query_norm, key_norm, precision=lax.Precision.HIGHEST)
        * score_scale
    )
    exponent = jnp.exp(scores)
    attn_weights = exponent / jnp.sum(exponent, -1, keepdims=True)
    return jnp.einsum("bhqk,bkhe->bqhe", attn_weights, value_rows, precision=lax.Precision.HIGHEST)


def cross_rows(left, right):
    return lax.dot_general(
        left, right, (((1,), (1,)), ((), ())), preferred_element_type=jnp.float32
    )


def over_tokens(left, right):
    return lax.dot_general(
        left, right, (((0,), (0,)), ((), ())), preferred_element_type=jnp.float32
    )


def body(tokens, weights, direction, precision):
    model_width = tokens.shape[1]
    local_rows = tokens.shape[0]
    share_rows = weights.shape[0]
    head_cols = weights.shape[2]
    normed = layer_norm(tokens.astype(jnp.float32)).astype(jnp.bfloat16)
    local = jnp.concatenate(
        [weights[:, 0:3], direction[:, 0:3], weights[:, 3:4], direction[:, 3:4]], 1
    ).reshape(share_rows, 8 * head_cols)
    gathered = lax.all_gather(local.T, FSDP, axis=1, tiled=True)
    in_both = gathered[: 6 * head_cols]
    out_both = gathered[6 * head_cols :]
    both_in = cross_rows(normed, in_both).astype(jnp.bfloat16)
    projected = both_in[:, : 3 * head_cols]
    tangent_in = both_in[:, 3 * head_cols :]

    def to_heads(block):
        return block.astype(jnp.float32).reshape(
            local_rows // PATCHES, PATCHES, 3, head_cols // HEAD, HEAD
        )

    primal = to_heads(projected)
    tangent_heads = to_heads(tangent_in)
    primal_args = (primal[:, :, 0], primal[:, :, 1], primal[:, :, 2])
    tangent_args = (tangent_heads[:, :, 0], tangent_heads[:, :, 1], tangent_heads[:, :, 2])
    mixed, mixed_dot = jax.jvp(attend, primal_args, tangent_args)
    mixed_rows = mixed.reshape(local_rows, head_cols).astype(jnp.bfloat16)
    tangent_out = mixed_dot.reshape(local_rows, head_cols).astype(jnp.bfloat16)
    partial_cols = lax.dot_general(
        out_both,
        jnp.concatenate([tangent_out, mixed_rows], 1),
        (((0,), (1,)), ((), ())),
        preferred_element_type=jnp.float32,
    )
    n_tensor = lax.axis_size(TENSOR)
    chunk = model_width // n_tensor
    n_core = lax.axis_size("core")
    n_chip = n_tensor // n_core
    swap = [(0, 1), (1, 0)]
    core_index = lax.axis_index("core")
    by_core = partial_cols.astype(jnp.bfloat16).reshape(n_chip, n_core, chunk, local_rows)
    kept = lax.dynamic_index_in_dim(by_core, core_index, 1, keepdims=False)
    given = lax.dynamic_index_in_dim(by_core, 1 - core_index, 1, keepdims=False)
    received = lax.ppermute(given, "core", swap)
    pair_sum = kept.astype(jnp.float32) + received.astype(jnp.float32)
    arrived = lax.all_to_all(pair_sum.astype(jnp.bfloat16), ("z_lo", "y"), 0, 0)
    output_dot = jnp.sum(arrived.astype(jnp.float32), 0)
    own_precision = lax.dynamic_slice_in_dim(precision, lax.axis_index(TENSOR) * chunk, chunk)
    cotangent_part = (own_precision[:, None] * output_dot).astype(jnp.bfloat16)
    spread = jnp.broadcast_to(cotangent_part[None], (n_chip, chunk, local_rows))
    on_chip = lax.all_to_all(spread, ("z_lo", "y"), 0, 0)
    partner = lax.ppermute(on_chip, "core", swap)
    first = core_index == 0
    cotangent_cols = jnp.stack(
        [jnp.where(first, on_chip, partner), jnp.where(first, partner, on_chip)], 1
    ).reshape(model_width, local_rows)
    back_rows = lax.dot_general(
        cotangent_cols,
        out_both[:head_cols],
        (((0,), (1,)), ((), ())),
        preferred_element_type=jnp.float32,
    )
    back_rows = back_rows.reshape(local_rows // PATCHES, PATCHES, head_cols // HEAD, HEAD)
    primal_out, pullback = jax.vjp(attend, *primal_args)
    gradients = pullback(back_rows)
    stacked = jnp.stack(gradients, axis=2).reshape(local_rows, 3 * head_cols).astype(jnp.bfloat16)
    summed = jnp.concatenate(
        [
            over_tokens(normed, stacked).reshape(model_width, 3, head_cols),
            jnp.dot(cotangent_cols, mixed_rows, preferred_element_type=jnp.float32)[:, None, :],
        ],
        axis=1,
    ).astype(jnp.bfloat16)
    n_hi = lax.axis_size("z_hi")
    n_x = lax.axis_size("x")
    summed = summed.reshape(n_hi, n_x, share_rows, 4, head_cols).swapaxes(0, 1)
    summed = summed.reshape(model_width, 4, head_cols)
    summed = lax.psum_scatter(summed, "x", scatter_dimension=0, tiled=True)
    blocks = summed.reshape(n_hi, share_rows, 4, head_cols)
    hi_index = lax.axis_index("z_hi")
    total = lax.dynamic_index_in_dim(blocks, hi_index, 0, keepdims=False).astype(jnp.float32)
    for shift in sorted(range(1, n_hi), key=lambda k: -min(k, n_hi - k)):
        outgoing = lax.dynamic_index_in_dim(blocks, (hi_index + shift) % n_hi, 0, keepdims=False)
        pairs = [(i, (i + shift) % n_hi) for i in range(n_hi)]
        total = total + lax.ppermute(outgoing, "z_hi", pairs).astype(jnp.float32)
    return total


def solution(mesh):
    n_fsdp, n_tensor = mesh.devices.shape
    n_x = 4 if n_fsdp % 4 == 0 else n_fsdp
    parts = mesh.devices.reshape(n_fsdp // n_x, n_x, 2, n_tensor // 4, 2)
    fine = Mesh(parts, ("z_hi", "x", "z_lo", "y", "core"))
    return jax.shard_map(
        body,
        mesh=fine,
        in_specs=(P(FSDP, None), P(FSDP, None, TENSOR), P(FSDP, None, TENSOR), P()),
        out_specs=P(FSDP, None, TENSOR),
        check_vma=False,
    )
```

profile of v0, /device:TPU:1, one launch (start us, length us, event | category | flops | bytes accessed | tf_op | source)
XLA Modules:
  0.0 423.0 jit_solution(7690654726230957890)
XLA Ops:
  12.1 3.2 copy.60
  16.7 2.5 fusion.5
  19.1 146.2 %all-gather.2.cloned.1.call-done = bf16[2048,3072]{0,1:T(8,128)(2,1)} async-done(((bf16[2048,192]{0,1:T(8,128)(2,1)}), bf16[2048,3072]{0,1:T(8,128)(2,1)}) %all-gather.2.cloned.1.call-update) | async-done | bytes 12582928 | tf_op jit(solution)/shard_map/all_gather | solution.py:53
  165.3 9.4 %fusion.10 = bf16[512,1536]{1,0:T(8,128)(2,1)S(1)} fusion(bf16[512,3072]{0,1:T(8,128)(2,1)} %fusion.5, bf16[2048,3072]{0,1:T(8,128)(2,1)} %all-gather.2.cloned.1.call-done), kind=kOutput, calls=%fused_computation.17 | convolution fusion | flops 4832624640 | bytes 14155776 | tf_op jit(solution)/shard_map/dot_general | solution.py:33
  192.5 3.7 convolution_convert_fusion
  199.2 3.4 collective-permute-done
  202.6 3.5 fusion.7
  206.1 14.4 %all-to-all-start = ((bf16[8,192,512]{2,1,0:T(8,128)(2,1)}), bf16[8,192,512]{2,1,0:T(8,128)(2,1)}, u32[]{:S(2)}, u32[]{:S(2)}) async-start(bf16[8,192,512]{2,1,0:T(8,128)(2,1)} %fusion.7), calls=%async_computation | async-start | bytes 3145728 | tf_op jit(solution)/shard_map/all_to_all | solution.py:89
  221.4 19.9 %all-to-all-done = bf16[8,192,512]{2,1,0:T(8,128)(2,1)} async-done(((bf16[8,192,512]{2,1,0:T(8,128)(2,1)}), bf16[8,192,512]{2,1,0:T(8,128)(2,1)}, u32[]{:S(2)}, u32[]{:S(2)}) %all-to-all-start) | async-done | bytes 1572896 | tf_op jit(solution)/shard_map/all_to_all | solution.py:89
  243.1 23.6 %all_to_all.10 = bf16[8,192,512]{2,1,0:T(8,128)(2,1)} all-to-all(bf16[8,192,512]{2,1,0:T(8,128)(2,1)S(1)} %broadcast_in_dim.12), channel_id=1, replica_groups=mesh['z_hi'=4,'x'=4,'z_lo'=2,'y'=4,'core'=2] {'z_lo','y'}, dimensions={0} | all-to-all | bytes 3145728 | tf_op jit(solution)/shard_map/all_to_all | solution.py:94
  266.7 2.4 collective-permute-start.1
  270.9 2.7 slice.71
  273.6 2.6 copy.78
  280.2 4.7 %copy.77 = bf16[512,3072]{1,0:T(8,128)(2,1)} copy(bf16[512,3072]{0,1:T(8,128)(2,1)} %bitcast.195) | data formatting | bytes 6291456 | tf_op jit(solution)/shard_map/dot_general | solution.py:100
  284.9 3.4 convolution_bitcast_fusion.2
  295.2 3.3 convert_element_type.93
  302.8 3.1 convolution_convert_fusion.1
  306.5 3.1 copy.87
  309.6 61.7 %reduce-scatter.2.cloned.1.call-done = bf16[768,4,256]{2,0,1:T(8,128)(2,1)} async-done(((bf16[3072,4,256]{2,0,1:T(8,128)(2,1)}), bf16[768,4,256]{2,0,1:T(8,128)(2,1)}) %reduce-scatter.2.cloned.1.call-update) | async-done | bytes 1572880 | tf_op jit(solution)/shard_map/reduce_scatter | solution.py:121
  373.8 5.5 %collective-permute-start.2 = (bf16[192,4,256]{2,1,0:T(4,128)(2,1)S(1)}, bf16[192,4,256]{2,1,0:T(4,128)(2,1)S(1)}, u32[]{:S(2)}, u32[]{:S(2)}) collective-permute-start(bf16[192,4,256]{2,1,0:T(4,128)(2,1)S(1)} %bitcast.214), channel_id=1, source_target_pairs={{0,128},{64,192},{128,0},{192,64},{1,129},{65,193},{129,1},{193,65... | collective-permute-start | bytes 1179656 | tf_op jit(solution)/shard_map/ppermute | solution.py:128
  379.8 3.1 collective-permute-start.4
  382.9 8.8 %collective-permute-done.2 = bf16[192,4,256]{2,1,0:T(4,128)(2,1)S(1)} collective-permute-done((bf16[192,4,256]{2,1,0:T(4,128)(2,1)S(1)}, bf16[192,4,256]{2,1,0:T(4,128)(2,1)S(1)}, u32[]{:S(2)}, u32[]{:S(2)}) %collective-permute-start.2) | collective-permute-done | bytes 393248 | tf_op jit(solution)/shard_map/ppermute | solution.py:128
  391.7 16.6 %collective-permute-done.3 = bf16[192,4,256]{2,1,0:T(4,128)(2,1)S(1)} collective-permute-done((bf16[192,4,256]{2,1,0:T(4,128)(2,1)S(1)}, bf16[192,4,256]{2,1,0:T(4,128)(2,1)S(1)}, u32[]{:S(2)}, u32[]{:S(2)}) %collective-permute-start.3) | collective-permute-done | bytes 393248 | tf_op jit(solution)/shard_map/ppermute | solution.py:128
  408.3 6.4 %collective-permute-done.4 = bf16[192,4,256]{2,1,0:T(4,128)(2,1)S(1)} collective-permute-done((bf16[192,4,256]{2,1,0:T(4,128)(2,1)S(1)}, bf16[192,4,256]{2,1,0:T(4,128)(2,1)S(1)}, u32[]{:S(2)}, u32[]{:S(2)}) %collective-permute-start.4) | collective-permute-done | bytes 393248 | tf_op jit(solution)/shard_map/ppermute | solution.py:128
  (82 shorter events, 52.1 us)
Async XLA Ops:
  6.5 158.8 %all-gather.2.cloned.1.call-start = ((), (), s32[]{:S(2)}) async-start(), calls=%async_computation.3 | async-start | bytes 13369344 | tf_op jit(solution)/shard_map/all_gather | solution.py:53
  176.1 1.7 copy-start.2
  196.2 2.2 copy-start.1
  198.4 4.2 collective-permute-start
  206.1 35.1 %all-to-all-start = ((bf16[8,192,512]{2,1,0:T(8,128)(2,1)}), bf16[8,192,512]{2,1,0:T(8,128)(2,1)}, u32[]{:S(2)}, u32[]{:S(2)}) async-start(bf16[8,192,512]{2,1,0:T(8,128)(2,1)} %fusion.7), calls=%async_computation | async-start | bytes 3145728 | tf_op jit(solution)/shard_map/all_to_all | solution.py:89
  220.5 150.8 %reduce-scatter.2.cloned.1.call-start = ((), (), s32[]{:S(2)}) async-start(), calls=%async_computation.4 | async-start | bytes 7864320 | tf_op jit(solution)/shard_map/reduce_scatter | solution.py:121
  266.7 9.5 %collective-permute-start.1 = (bf16[8,192,512]{2,1,0:T(8,128)(2,1)}, bf16[8,192,512]{2,1,0:T(8,128)(2,1)}, u32[]{:S(2)}, u32[]{:S(2)}) collective-permute-start(bf16[8,192,512]{2,1,0:T(8,128)(2,1)} %all_to_all.10), channel_id=1, source_target_pairs={{0,1},{1,0},{2,3},{3,2},{4,5},{5,4},{6,7},{7,6},{8,9},{9,8},{10,11... | collective-permute-start | bytes 4718600 | tf_op jit(solution)/shard_map/ppermute | solution.py:95
  293.3 7.4 %copy-start.4 = (bf16[512,256,1,1]{1,0,2,3:T(8,128)(2,1)S(1)}, bf16[512,256,1,1]{1,0,2,3:T(8,128)(2,1)}, u32[]{:S(2)}) copy-start(bf16[512,256,1,1]{1,0,2,3:T(8,128)(2,1)} %reshape.188) | copy-start | bytes 786436
  295.2 5.6 %copy-start = (bf16[8,2,192,512]{3,2,1,0:T(8,128)(2,1)S(1)}, bf16[8,2,192,512]{3,2,1,0:T(8,128)(2,1)}, u32[]{:S(2)}) copy-start(bf16[8,2,192,512]{3,2,1,0:T(8,128)(2,1)} %pad_maximum_fusion) | copy-start | bytes 9437188
  300.7 1.9 copy-start.3
  300.7 2.1 copy-start.5
  373.8 18.0 %collective-permute-start.2 = (bf16[192,4,256]{2,1,0:T(4,128)(2,1)S(1)}, bf16[192,4,256]{2,1,0:T(4,128)(2,1)S(1)}, u32[]{:S(2)}, u32[]{:S(2)}) collective-permute-start(bf16[192,4,256]{2,1,0:T(4,128)(2,1)S(1)} %bitcast.214), channel_id=1, source_target_pairs={{0,128},{64,192},{128,0},{192,64},{1,129},{65,193},{129,1},{193,65... | collective-permute-start | bytes 1179656 | tf_op jit(solution)/shard_map/ppermute | solution.py:128
  379.3 29.0 %collective-permute-start.3 = (bf16[192,4,256]{2,1,0:T(4,128)(2,1)S(1)}, bf16[192,4,256]{2,1,0:T(4,128)(2,1)S(1)}, u32[]{:S(2)}, u32[]{:S(2)}) collective-permute-start(bf16[192,4,256]{2,1,0:T(4,128)(2,1)S(1)} %bitcast.213), channel_id=1, source_target_pairs={{0,64},{64,128},{128,192},{192,0},{1,65},{65,129},{129,193},{193,1... | collective-permute-start | bytes 1179656 | tf_op jit(solution)/shard_map/ppermute | solution.py:128
  379.8 35.0 %collective-permute-start.4 = (bf16[192,4,256]{2,1,0:T(4,128)(2,1)S(1)}, bf16[192,4,256]{2,1,0:T(4,128)(2,1)S(1)}, u32[]{:S(2)}, u32[]{:S(2)}) collective-permute-start(bf16[192,4,256]{2,1,0:T(4,128)(2,1)S(1)} %bitcast.212), channel_id=1, source_target_pairs={{0,192},{64,0},{128,64},{192,128},{1,193},{65,1},{129,65},{193,129... | collective-permute-start | bytes 1179656 | tf_op jit(solution)/shard_map/ppermute | solution.py:128
Sparse Core Ops, SparseCore 0:
  12.2 153.0 all-gather.1
  309.7 61.5 reduce-scatter.1
where the time goes:
time: 424 us; the launch traced here: 423 us
  waiting for transfers between devices  263 us (62%)
  local copies, waits for them, and re-layouts  44.5 us (10%)
  matrix products  32.8 us (8%)
  starting transfers between devices  26.8 us (6%)
  blocking collectives  23.6 us (6%)
  other arithmetic  18.5 us (4%)
  between operations  13.8 us (3%)
    all_gather x1, waiting for transfers between devices, body(): gathered = lax.all_gather(local.T, FSDP, axis=1, tiled=True)  146 us
    reduce_scatter x1, waiting for transfers between devices, body(): summed = lax.psum_scatter(summed, 'x', scatter_dimension=0, tiled=True)  61.7 us
    ppermute x3, waiting for transfers between devices, body(): total = total + lax.ppermute(outgoing, 'z_hi', pairs).astype(jnp.float32)  31.9 us
    all_to_all x1, blocking collectives, body(): on_chip = lax.all_to_all(spread, ('z_lo', 'y'), 0, 0)  23.6 us
    all_to_all x1, waiting for transfers between devices, body(): arrived = lax.all_to_all(pair_sum.astype(jnp.bfloat16), ('z_lo', 'y'), 0, 0)  19.9 us
    all_to_all x1, starting transfers between devices, body(): arrived = lax.all_to_all(pair_sum.astype(jnp.bfloat16), ('z_lo', 'y'), 0, 0)  14.4 us
    dot_general x1, matrix products, cross_rows(): lax.dot_general(left, right, (((1,), (1,)), ((), ())), preferred_element_...  9.42 us
    ppermute x3, starting transfers between devices, body(): total = total + lax.ppermute(outgoing, 'z_hi', pairs).astype(jnp.float32)  9.12 us
  transfers between devices with their start and end apart: 8, of which 7 were waited for; matrix products, arithmetic and copies ran while one was open for 4% of the time, Pallas kernels for 0%

commit v1 on v0

--- a/solution.py
+++ b/solution.py
@@ -50,7 +50,9 @@
     local = jnp.concatenate(
         [weights[:, 0:3], direction[:, 0:3], weights[:, 3:4], direction[:, 3:4]], 1
     ).reshape(share_rows, 8 * head_cols)
-    gathered = lax.all_gather(local.T, FSDP, axis=1, tiled=True)
+    gathered = jnp.concatenate(
+        lax.all_to_all(jnp.stack([local.T] * lax.axis_size(FSDP)), FSDP, 0, 0), axis=1
+    )
     in_both = gathered[: 6 * head_cols]
     out_both = gathered[6 * head_cols :]
     both_in = cross_rows(normed, in_both).astype(jnp.bfloat16)

time: 424 us -> 592 us (1.40); the launches traced: 423 us -> 584 us
  waiting for transfers between devices: 263 us -> 379 us
  starting transfers between devices: 26.8 us -> 48.9 us
  local copies, waits for them, and re-layouts: 44.5 us -> 65.5 us
    all_to_all x0 -> x1, waiting for transfers between devices: none -> 258 us  [body(): lax.all_to_all(jnp.stack([local.T] * lax.axis_size(FSDP)), FSDP, 0, 0)]
    all_gather x1 -> x0, waiting for transfers between devices: 146 us -> none  [body(): gathered = lax.all_gather(local.T, FSDP, axis=1, tiled=True)]
    slice x0 -> x2, local copies, waits for them, and re-layouts: none -> 12.1 us  [the longest x1 8.23 us: body(): in_both = gathered[:6 * head_cols]]
    all_to_all x0 -> x1, starting transfers between devices: none -> 11.6 us  [body(): lax.all_to_all(jnp.stack([local.T] * lax.axis_size(FSDP)), FSDP, 0, 0)]
    all_to_all x1, starting transfers between devices: 14.4 us -> 23.6 us  [body(): arrived = lax.all_to_all(pair_sum.astype(jnp.bfloat16), ('z_lo', 'y'), 0, 0)]
    dot_general x1 -> x3, local copies, waits for them, and re-layouts: 4.69 us -> 13.4 us  [body(): lax.dot_general(cotangent_cols, out_both[:head_cols], (((0,), (1,)), ((),...]
    another operation x0 -> x1, local copies, waits for them, and re-layouts: none -> 6.08 us  [body(): jnp.stack([local.T] * lax.axis_size(FSDP))]
where the time goes in v1:
time: 592 us; the launch traced here: 584 us
  waiting for transfers between devices  379 us (64%)
  local copies, waits for them, and re-layouts  65.5 us (11%)
  starting transfers between devices  48.9 us (8%)
  matrix products  32.8 us (6%)
  blocking collectives  23.6 us (4%)
  other arithmetic  19.7 us (3%)
  between operations  14.1 us (2%)
    all_to_all x1, waiting for transfers between devices, body(): lax.all_to_all(jnp.stack([local.T] * lax.axis_size(FSDP)), FSDP, 0, 0)  258 us
    reduce_scatter x1, waiting for transfers between devices, body(): summed = lax.psum_scatter(summed, 'x', scatter_dimension=0, tiled=True)  67 us
    ppermute x3, waiting for transfers between devices, body(): total = total + lax.ppermute(outgoing, 'z_hi', pairs).astype(jnp.float32)  31.1 us
    all_to_all x1, blocking collectives, body(): on_chip = lax.all_to_all(spread, ('z_lo', 'y'), 0, 0)  23.6 us
    all_to_all x1, starting transfers between devices, body(): arrived = lax.all_to_all(pair_sum.astype(jnp.bfloat16), ('z_lo', 'y'), 0, 0)  23.6 us
    all_to_all x1, waiting for transfers between devices, body(): arrived = lax.all_to_all(pair_sum.astype(jnp.bfloat16), ('z_lo', 'y'), 0, 0)  19.9 us
    dot_general x3, local copies, waits for them, and re-layouts, body(): lax.dot_general(cotangent_cols, out_both[:head_cols], (((0,), (1,)), ((),...  13.4 us
  transfers between devices with their start and end apart: 8, of which 7 were waited for; matrix products, arithmetic and copies ran while one was open for 4% of the time, Pallas kernels for 0%

profile of v1, /device:TPU:1, one launch (start us, length us, event | category | flops | bytes accessed | tf_op | source)
XLA Modules:
  0.0 584.0 jit_solution(16282878200279378111)
XLA Ops:
  11.2 6.1 %stack.20 = bf16[16,2048,192]{1,2,0:T(8,128)(2,1)} broadcast(bf16[2048,192]{0,1:T(8,128)(2,1)S(1)} %bitcast.207), dimensions={1,2} | broadcast | bytes 13369344 | tf_op jit(solution)/shard_map/stack | solution.py:54
  17.3 11.6 %all-to-all-start = ((bf16[16,2048,192]{1,2,0:T(8,128)(2,1)}), bf16[16,2048,192]{1,2,0:T(8,128)(2,1)}, u32[]{:S(2)}, u32[]{:S(2)}) async-start(bf16[16,2048,192]{1,2,0:T(8,128)(2,1)} %stack.20), calls=%async_computation | async-start | bytes 25165824 | tf_op jit(solution)/shard_map/all_to_all | solution.py:54
  28.9 3.2 copy.28
  36.0 258.1 %all-to-all-done = bf16[16,2048,192]{1,2,0:T(8,128)(2,1)} async-done(((bf16[16,2048,192]{1,2,0:T(8,128)(2,1)}), bf16[16,2048,192]{1,2,0:T(8,128)(2,1)}, u32[]{:S(2)}, u32[]{:S(2)}) %all-to-all-start) | async-done | bytes 12582944 | tf_op jit(solution)/shard_map/all_to_all | solution.py:54
  294.1 8.2 %slice.71 = bf16[1536,16,192]{0,2,1:T(8,128)(2,1)} slice(bf16[2048,16,192]{0,2,1:T(8,128)(2,1)} %bitcast.5), slice={[0:1536], [0:16], [0:192]} | slice | bytes 18874368 | tf_op jit(solution)/shard_map/slice | solution.py:56
  302.4 7.8 %convolution_convert_fusion.1 = bf16[512,1536]{1,0:T(8,128)(2,1)S(1)} fusion(bf16[512,3072]{0,1:T(8,128)(2,1)S(1)} %copy-done.2, bf16[1536,3072]{0,1:T(8,128)(2,1)} %bitcast.206), kind=kOutput, calls=%fused_computation.14 | convolution fusion | flops 4832624640 | bytes 14155776 | tf_op jit(solution)/shard_map/dot_general | solution.py:33
  322.9 3.8 slice.70
  336.9 3.7 convolution_convert_fusion
  344.8 3.4 collective-permute-done
  348.2 3.6 fusion.4
  351.8 23.6 %all-to-all-start.1 = ((bf16[8,192,512]{2,1,0:T(8,128)(2,1)}), bf16[8,192,512]{2,1,0:T(8,128)(2,1)}, u32[]{:S(2)}, u32[]{:S(2)}) async-start(bf16[8,192,512]{2,1,0:T(8,128)(2,1)} %fusion.4), calls=%async_computation.1 | async-start | bytes 3145728 | tf_op jit(solution)/shard_map/all_to_all | solution.py:91
  376.2 19.9 %all-to-all-done.1 = bf16[8,192,512]{2,1,0:T(8,128)(2,1)} async-done(((bf16[8,192,512]{2,1,0:T(8,128)(2,1)}), bf16[8,192,512]{2,1,0:T(8,128)(2,1)}, u32[]{:S(2)}, u32[]{:S(2)}) %all-to-all-start.1) | async-done | bytes 1572896 | tf_op jit(solution)/shard_map/all_to_all | solution.py:91
  397.9 23.6 %all_to_all.15 = bf16[8,192,512]{2,1,0:T(8,128)(2,1)} all-to-all(bf16[8,192,512]{2,1,0:T(8,128)(2,1)S(1)} %broadcast_in_dim.12), channel_id=1, replica_groups=mesh['z_hi'=4,'x'=4,'z_lo'=2,'y'=4,'core'=2] {'z_lo','y'}, dimensions={0} | all-to-all | bytes 3145728 | tf_op jit(solution)/shard_map/all_to_all | solution.py:96
  428.4 3.7 dot_general.76
  432.2 5.0 copy.46
  441.2 4.7 copy.45
  445.9 3.4 fusion.18
  456.3 4.7 convolution_convert_fusion.2
  465.7 67.0 %reduce-scatter.2.cloned.1.call-done = bf16[768,4,256]{2,0,1:T(8,128)(2,1)} async-done(((bf16[3072,4,256]{2,0,1:T(8,128)(2,1)}), bf16[768,4,256]{2,0,1:T(8,128)(2,1)}) %reduce-scatter.2.cloned.1.call-update) | async-done | bytes 1572880 | tf_op jit(solution)/shard_map/reduce_scatter | solution.py:123
  534.5 5.5 collective-permute-start.2
  541.2 3.2 collective-permute-start.4
  544.3 7.9 %collective-permute-done.2 = bf16[192,4,256]{2,1,0:T(4,128)(2,1)S(1)} collective-permute-done((bf16[192,4,256]{2,1,0:T(4,128)(2,1)S(1)}, bf16[192,4,256]{2,1,0:T(4,128)(2,1)S(1)}, u32[]{:S(2)}, u32[]{:S(2)}) %collective-permute-start.2) | collective-permute-done | bytes 393248 | tf_op jit(solution)/shard_map/ppermute | solution.py:130
  552.2 14.3 %collective-permute-done.3 = bf16[192,4,256]{2,1,0:T(4,128)(2,1)S(1)} collective-permute-done((bf16[192,4,256]{2,1,0:T(4,128)(2,1)S(1)}, bf16[192,4,256]{2,1,0:T(4,128)(2,1)S(1)}, u32[]{:S(2)}, u32[]{:S(2)}) %collective-permute-start.3) | collective-permute-done | bytes 393248 | tf_op jit(solution)/shard_map/ppermute | solution.py:130
  566.5 8.9 %collective-permute-done.4 = bf16[192,4,256]{2,1,0:T(4,128)(2,1)S(1)} collective-permute-done((bf16[192,4,256]{2,1,0:T(4,128)(2,1)S(1)}, bf16[192,4,256]{2,1,0:T(4,128)(2,1)S(1)}, u32[]{:S(2)}, u32[]{:S(2)}) %collective-permute-start.4) | collective-permute-done | bytes 393248 | tf_op jit(solution)/shard_map/ppermute | solution.py:130
  (81 shorter events, 65.1 us)
Async XLA Ops:
  17.3 276.9 %all-to-all-start = ((bf16[16,2048,192]{1,2,0:T(8,128)(2,1)}), bf16[16,2048,192]{1,2,0:T(8,128)(2,1)}, u32[]{:S(2)}, u32[]{:S(2)}) async-start(bf16[16,2048,192]{1,2,0:T(8,128)(2,1)} %stack.20), calls=%async_computation | async-start | bytes 25165824 | tf_op jit(solution)/shard_map/all_to_all | solution.py:54
  294.1 8.2 %copy-start.2 = (bf16[512,3072]{0,1:T(8,128)(2,1)S(1)}, bf16[512,3072]{0,1:T(8,128)(2,1)}, u32[]{:S(2)}) copy-start(bf16[512,3072]{0,1:T(8,128)(2,1)} %fusion.3) | copy-start | bytes 9437188
  340.6 2.2 copy-start.1
  342.9 5.4 collective-permute-start
  351.8 44.2 %all-to-all-start.1 = ((bf16[8,192,512]{2,1,0:T(8,128)(2,1)}), bf16[8,192,512]{2,1,0:T(8,128)(2,1)}, u32[]{:S(2)}, u32[]{:S(2)}) async-start(bf16[8,192,512]{2,1,0:T(8,128)(2,1)} %fusion.4), calls=%async_computation.1 | async-start | bytes 3145728 | tf_op jit(solution)/shard_map/all_to_all | solution.py:91
  375.3 157.3 %reduce-scatter.2.cloned.1.call-start = ((), (), s32[]{:S(2)}) async-start(), calls=%async_computation.4 | async-start | bytes 7864320 | tf_op jit(solution)/shard_map/reduce_scatter | solution.py:123
  421.5 15.6 %collective-permute-start.1 = (bf16[8,192,512]{2,1,0:T(8,128)(2,1)}, bf16[8,192,512]{2,1,0:T(8,128)(2,1)}, u32[]{:S(2)}, u32[]{:S(2)}) collective-permute-start(bf16[8,192,512]{2,1,0:T(8,128)(2,1)} %all_to_all.15), channel_id=1, source_target_pairs={{0,1},{1,0},{2,3},{3,2},{4,5},{5,4},{6,7},{7,6},{8,9},{9,8},{10,11... | collective-permute-start | bytes 4718600 | tf_op jit(solution)/shard_map/ppermute | solution.py:97
  456.3 4.7 copy-start
  456.3 4.7 copy-start.3
  534.5 17.8 %collective-permute-start.2 = (bf16[192,4,256]{2,1,0:T(4,128)(2,1)S(1)}, bf16[192,4,256]{2,1,0:T(4,128)(2,1)S(1)}, u32[]{:S(2)}, u32[]{:S(2)}) collective-permute-start(bf16[192,4,256]{2,1,0:T(4,128)(2,1)S(1)} %bitcast.221), channel_id=1, source_target_pairs={{0,128},{64,192},{128,0},{192,64},{1,129},{65,193},{129,1},{193,65... | collective-permute-start | bytes 1179656 | tf_op jit(solution)/shard_map/ppermute | solution.py:130
  540.3 26.2 %collective-permute-start.3 = (bf16[192,4,256]{2,1,0:T(4,128)(2,1)S(1)}, bf16[192,4,256]{2,1,0:T(4,128)(2,1)S(1)}, u32[]{:S(2)}, u32[]{:S(2)}) collective-permute-start(bf16[192,4,256]{2,1,0:T(4,128)(2,1)S(1)} %bitcast.222), channel_id=1, source_target_pairs={{0,64},{64,128},{128,192},{192,0},{1,65},{65,129},{129,193},{193,1... | collective-permute-start | bytes 1179656 | tf_op jit(solution)/shard_map/ppermute | solution.py:130
  541.2 34.3 %collective-permute-start.4 = (bf16[192,4,256]{2,1,0:T(4,128)(2,1)S(1)}, bf16[192,4,256]{2,1,0:T(4,128)(2,1)S(1)}, u32[]{:S(2)}, u32[]{:S(2)}) collective-permute-start(bf16[192,4,256]{2,1,0:T(4,128)(2,1)S(1)} %bitcast.223), channel_id=1, source_target_pairs={{0,192},{64,0},{128,64},{192,128},{1,193},{65,1},{129,65},{193,129... | collective-permute-start | bytes 1179656 | tf_op jit(solution)/shard_map/ppermute | solution.py:130
Sparse Core Ops, SparseCore 0:
  465.8 66.8 reduce-scatter.1
